TPU v7x, 32 devices: a whole 2x2x4 slice. The times are simulated.
32 devices in a mesh: row: 8 (over z, y), col: 4 (over x, core).
Axes of the slice: x: 2, y: 2, z: 4, core: 2. Of those that a mesh axis runs over, the one named last changes fastest.
Arguments:
- density: float32 [4, 256, 2048], P('col', 'row'), may hold values from 0.5 to 2
- momentum: float32 [3, 4, 256, 2048], P(None, 'col', 'row'), may hold values from -6 to 6
- energy: float32 [4, 256, 2048], P('col', 'row'), may hold values from 2 to 5
Outputs:
- tendency: float32 [5, 4, 256, 2048], P(None, 'col', 'row')
All inputs are finite; a program needn't handle non-finite values.
Results may differ from a plain program's by a relative error of at most 0.000053.
Values sent between devices are 32-bit elements; how exact they have to be, the bound alone decides.
No kernel may reach another device: no remote copies, remote signals or barrier semaphores. Data moves between devices by JAX's collectives and lax.ppermute only.
A program may use at most 64 MiB of HBM per device.

v0:
```python
import jax
import jax.numpy as jnp
import numpy as np
from jax import lax
from jax.sharding import PartitionSpec as P


def operator_column(count):
    steps = np.arange(count)
    wave = 2.0 * np.pi * steps / count
    upper = (
        17.0 / 12.0 * np.sin(wave)
        + 101.0 / 300.0 * np.sin(2.0 * wave)
        + 1.0 / 300.0 * np.sin(3.0 * wave)
    )
    lower = 1.0 + np.cos(wave) + 0.1 * np.cos(2.0 * wave)
    ratio = upper / lower
    phase = 2.0 * np.pi * (steps[:, None] * steps[None, :] % count) / count
    return -np.sum(ratio[:, None] * np.sin(phase), axis=0) / count


def operator_table(count):
    column = operator_column(count)
    steps = np.arange(count)
    offsets = (steps[None, :] - steps[:, None]) % count
    return column[offsets].astype(np.float32)


def block_weights(count):
    table = operator_table(count)
    width = 128
    w_self = table[:width, :width]
    w_prev = table[:width, width : 2 * width]
    w_next = table[width : 2 * width, :width]
    return jnp.asarray(np.concatenate([w_prev, w_self, w_next], axis=1))


def compact_last(field):
    count = field.shape[-1]
    width = 128
    blocks = field.reshape(field.shape[:-1] + (count // width, width))
    parts = jnp.einsum(
        "...bj,jk->...bk", blocks, block_weights(count), precision=lax.Precision.HIGHEST
    )
    result = (
        jnp.roll(parts[..., :width], 1, axis=-2)
        + parts[..., width : 2 * width]
        + jnp.roll(parts[..., 2 * width :], -1, axis=-2)
    )
    return result.reshape(field.shape)


def compact_second(field):
    count = field.shape[-2]
    if count <= 256:
        weights = jnp.asarray(operator_table(count))
        return jnp.einsum("...jc,ji->...ic", field, weights, precision=lax.Precision.HIGHEST)
    width = 128
    blocks = field.reshape(field.shape[:-2] + (count // width, width, field.shape[-1]))
    parts = jnp.einsum(
        "...bjc,jk->...bkc", blocks, block_weights(count), precision=lax.Precision.HIGHEST
    )
    result = (
        jnp.roll(parts[..., :width, :], 1, axis=-3)
        + parts[..., width : 2 * width, :]
        + jnp.roll(parts[..., 2 * width :, :], -1, axis=-3)
    )
    return result.reshape(field.shape)


def fluxes(density, momentum, energy):
    speed = momentum / density[None]
    pressure = 0.4 * (energy - 0.5 * jnp.sum(momentum * momentum, axis=0) / density)
    enthalpy = energy + pressure
    vel_x, vel_y = (speed[0], speed[1])
    flux_x = jnp.stack(
        [
            momentum[0],
            momentum[0] * vel_x + pressure,
            momentum[1] * vel_x,
            momentum[2] * vel_x,
            enthalpy * vel_x,
        ]
    )
    flux_y = jnp.stack(
        [
            momentum[1],
            momentum[0] * vel_y,
            momentum[1] * vel_y + pressure,
            momentum[2] * vel_y,
            enthalpy * vel_y,
        ],
        axis=2,
    )
    return (flux_x, flux_y)


def local(density, momentum, energy):
    flux_x, flux_y = fluxes(density, momentum, energy)
    planes, owned, length = (flux_y.shape[0], flux_y.shape[1], flux_y.shape[3])
    packed = flux_y.reshape(planes, owned, 5 * length)
    derivative_x = compact_last(flux_x)
    y_lines = lax.all_to_all(packed, "row", split_axis=2, concat_axis=1, tiled=True)
    derivative_lines = compact_second(y_lines)
    derived = lax.all_to_all(derivative_lines, "row", split_axis=1, concat_axis=2, tiled=True)
    derivative_y = jnp.transpose(derived.reshape(planes, owned, 5, length), (2, 0, 1, 3))
    return -(derivative_x + derivative_y)


def solution(mesh):
    in_specs = (P("col", "row", None), P(None, "col", "row", None), P("col", "row", None))
    out_specs = P(None, "col", "row", None)
    return jax.shard_map(local, mesh=mesh, in_specs=in_specs, out_specs=out_specs, check_vma=False)
```

profile of v0, /device:TPU:0, one launch (start us, length us, event | category | flops | bytes accessed | tf_op | source)
XLA Modules:
  0.0 174.0 jit_solution(4821467168655819884)
XLA Ops:
  0.0 1.0 bitcast_dynamic-update-slice_fusion.9
  1.1 1.4 multiply_reduce_fusion
  2.7 3.8 %copy.31 = f32[1,32,5,2048]{1,3,2,0:T(8,128)} copy(f32[1,32,5,2048]{3,1,2,0:T(8,128)S(1)} %bitcast_dynamic-update-slice_fusion.5) | data formatting | bytes 2621440 | tf_op jit(solution)/shard_map/reshape | solution.py:101
  6.5 0.5 broadcast.11
  7.0 47.4 %reduce.1 = f32[10240,32]{1,0:T(8,128)} reduce(f32[10240,1,32]{2,1,0:T(1,128)} %bitcast.106, f32[]{:T(128)} %broadcast.11), dimensions={1}, to_apply=%bitcast.93.reduce_sub_computation | reduce | bytes 2621444
  54.4 5.3 %reshape.146 = f32[8,1,40960]{2,1,0:T(1,128)} reshape(f32[10240,32]{1,0:T(8,128)} %reduce.1) | data formatting | bytes 2621440
  59.8 38.7 %all_to_all.30 = f32[8,1,40960]{2,1,0:T(1,128)S(1)} all-to-all(f32[8,1,40960]{2,1,0:T(1,128)} %reshape.146), channel_id=1, replica_groups=mesh['row'=8,'col'=4] {'row'}, dimensions={0} | all-to-all | bytes 2621440 | tf_op jit(solution)/shard_map/all_to_all | solution.py:103
  98.4 5.2 %reduce.2 = f32[8,40960]{1,0:T(8,128)} reduce(f32[8,1,40960]{2,1,0:T(1,128)S(1)} %all_to_all.30, f32[]{:T(128)} %broadcast.11), dimensions={1}, to_apply=%all_to_all.22.reduce_sub_computation | reduce | bytes 2621444 | tf_op jit(solution)/shard_map/all_to_all | solution.py:103
  103.7 12.0 %reshape.147 = f32[10240,1,32]{2,1,0:T(1,128)} reshape(f32[8,40960]{1,0:T(8,128)} %reduce.2) | data formatting | bytes 2621440
  115.6 10.6 %copy.26 = f32[1,32,10240]{2,1,0:T(8,128)} copy(f32[1,32,10240]{1,0,2:T(1,128)} %bitcast.107) | data formatting | bytes 2621440 | tf_op jit(solution)/shard_map/all_to_all | solution.py:103
  126.2 1.5 reshape.141
  127.8 2.2 %convolution_bitcast_fusion = f32[1,256,1280]{2,1,0:T(8,128)S(1)} fusion(f32[256,256]{1,0:T(8,128)} %constant.17, f32[256,1280]{1,0:T(8,128)S(1)} %reshape.141), kind=kOutput, calls=%fused_computation | convolution fusion | flops 1006632960 | bytes 2883584 | tf_op jit(solution)/shard_map/...jc,ji->...ic/dot_general | solution.py:57
  130.0 2.4 %copy.27 = f32[1,256,1280]{2,0,1:T(1,128)} copy(f32[1,256,1280]{2,1,0:T(8,128)S(1)} %convolution_bitcast_fusion) | data formatting | bytes 2621440 | tf_op jit(solution)/shard_map/...jc,ji->...ic/transpose | solution.py:57
  132.4 4.3 %all-to-all-start.1 = ((f32[1,256,1280]{2,0,1:T(1,128)}), f32[1,256,1280]{2,0,1:T(1,128)}, u32[]{:S(2)}, u32[]{:S(2)}) async-start(f32[1,256,1280]{2,0,1:T(1,128)} %copy.27), calls=%async_computation.1 | async-start | bytes 2621440 | tf_op jit(solution)/shard_map/all_to_all | solution.py:105
  137.2 0.8 copy-done.3
  138.0 3.5 %convolution_bitcast_fusion.1 = f32[5,1,32,16,384]{4,3,2,0,1:T(8,128)S(1)} fusion(f32[5,32,16,128]{3,2,1,0:T(8,128)S(1)} %bitcast_dynamic-update-slice_fusion, f32[128,384,1,1]{1,0,3,2:T(8,128)S(1)} %copy-done.3), kind=kOutput, calls=%fused_computation.1 | convolution fusion | flops 1509949440 | bytes 5439488 | tf_op jit(solution)/shard_map/...bj,jk->...bk/dot_general | solution.py:42
  141.5 0.1 fusion.10
  141.6 0.2 fusion.9
  141.9 0.4 fusion
  142.2 0.2 reshape.137
  142.4 24.9 %all-to-all-done.1 = f32[1,256,1280]{2,0,1:T(1,128)} async-done(((f32[1,256,1280]{2,0,1:T(1,128)}), f32[1,256,1280]{2,0,1:T(1,128)}, u32[]{:S(2)}, u32[]{:S(2)}) %all-to-all-start.1) | async-done | bytes 1310752 | tf_op jit(solution)/shard_map/all_to_all | solution.py:105
  167.3 3.1 %copy.40 = f32[1,8,32,1280]{3,1,2,0:T(8,128)} copy(f32[1,8,32,1280]{3,0,2,1:T(1,128)} %bitcast.16) | data formatting | bytes 2621440 | tf_op jit(solution)/shard_map/all_to_all | solution.py:105
  170.5 1.5 reshape.140
  172.0 2.0 %fusion.1 = f32[5,1,32,2048]{3,2,1,0:T(8,128)} fusion(f32[5,1,32,2048]{3,2,1,0:T(8,128)S(1)} %reshape.137, f32[1,32,5,2048]{3,2,1,0:T(8,128)S(1)} %reshape.140), kind=kLoop, calls=%fused_computation.5 | loop fusion | flops 655360 | bytes 3932160 | tf_op jit(solution)/shard_map/neg | solution.py:107
  (23 shorter events, 0.7 us)
Async XLA Ops:
  0.0 2.5 %copy-start = (f32[3,1,32,2048]{3,2,1,0:T(8,128)S(1)}, f32[3,1,32,2048]{3,2,1,0:T(8,128)}, u32[]{:S(2)}) copy-start(f32[3,1,32,2048]{3,2,1,0:T(8,128)} %param.6) | copy-start | bytes 2359300
  1.0 1.5 copy-start.1
  1.1 1.5 copy-start.2
  132.4 35.0 %all-to-all-start.1 = ((f32[1,256,1280]{2,0,1:T(1,128)}), f32[1,256,1280]{2,0,1:T(1,128)}, u32[]{:S(2)}, u32[]{:S(2)}) async-start(f32[1,256,1280]{2,0,1:T(1,128)} %copy.27), calls=%async_computation.1 | async-start | bytes 2621440 | tf_op jit(solution)/shard_map/all_to_all | solution.py:105
  137.1 0.9 copy-start.3
where the time goes:
time: 175 us; the launch traced here: 174 us
  other arithmetic  56.7 us (32%)
  local copies, waits for them, and re-layouts  43.5 us (25%)
  blocking collectives  38.7 us (22%)
  waiting for transfers between devices  24.9 us (14%)
  matrix products  5.71 us (3%)
  starting transfers between devices  4.26 us (2%)
    unnamed x6, other arithmetic  47.7 us
    all_to_all x1, blocking collectives, local(): lax.all_to_all(packed, 'row', split_axis=2, concat_axis=1, tiled=True)  38.7 us
    all_to_all x1, waiting for transfers between devices, local(): lax.all_to_all(derivative_lines, 'row', split_axis=1, concat_axis=2, tile...  24.9 us
    unnamed x21, local copies, waits for them, and re-layouts  20 us
    all_to_all x1, local copies, waits for them, and re-layouts, local(): lax.all_to_all(packed, 'row', split_axis=2, concat_axis=1, tiled=True)  10.6 us
    all_to_all x1, other arithmetic, local(): lax.all_to_all(packed, 'row', split_axis=2, concat_axis=1, tiled=True)  5.24 us
    all_to_all x1, starting transfers between devices, local(): lax.all_to_all(derivative_lines, 'row', split_axis=1, concat_axis=2, tile...  4.26 us
    reshape x1, local copies, waits for them, and re-layouts, local(): packed = flux_y.reshape(planes, owned, 5 * length)  3.76 us
  transfers between devices with their start and end apart: 1, of which 1 were waited for; matrix products, arithmetic and copies ran while one was open for 3% of the time, Pallas kernels for 0%

commit v1 on v0

--- a/solution.py
+++ b/solution.py
@@ -3,6 +3,34 @@
 import numpy as np
 from jax import lax
 from jax.sharding import PartitionSpec as P
+
+
+def _tell_quarters(page, on_dim, xs):
+    mixed_arr, f_now = (page.shape[:on_dim], page.shape[on_dim + 1 :])
+    return jnp.moveaxis(page.reshape(*mixed_arr, xs, -1, *f_now), on_dim, 0)
+
+
+def switch_scales_in(x_in, d0):
+    x_in = jnp.moveaxis(x_in, 0, d0)
+    w1 = x_in.shape
+    return x_in.reshape(*w1[:d0], w1[d0] * w1[d0 + 1], *w1[d0 + 2 :])
+
+
+def tables_direct(block_in, mesh_ax, x0, local_x):
+    w2 = jax.lax.axis_size(mesh_ax)
+    state_next = jax.lax.axis_index(mesh_ax)
+    new, block_last = (w2, state_next)
+    response = _tell_quarters(local_x, x0, new)
+    next_value = response
+    for m in range(1, new):
+        kept_arr, passed = ((block_last + m) % new, (block_last - m) % new)
+        met_up = lax.dynamic_index_in_dim(response, kept_arr, 0)
+        block_list = []
+        for h in range(new):
+            block_list.append((h, (h + m) % new))
+        back = jax.lax.ppermute(met_up, axis_name=mesh_ax, perm=block_list)
+        next_value = lax.dynamic_update_slice_in_dim(next_value, back, passed, axis=0)
+    return switch_scales_in(next_value, block_in)
 
 
 def operator_column(count):
@@ -100,7 +128,7 @@
     planes, owned, length = (flux_y.shape[0], flux_y.shape[1], flux_y.shape[3])
     packed = flux_y.reshape(planes, owned, 5 * length)
     derivative_x = compact_last(flux_x)
-    y_lines = lax.all_to_all(packed, "row", split_axis=2, concat_axis=1, tiled=True)
+    y_lines = tables_direct(1, "row", 2, packed)
     derivative_lines = compact_second(y_lines)
     derived = lax.all_to_all(derivative_lines, "row", split_axis=1, concat_axis=2, tiled=True)
     derivative_y = jnp.transpose(derived.reshape(planes, owned, 5, length), (2, 0, 1, 3))

time: 175 us -> 114 us (0.65)
  other arithmetic: 56.7 us -> 5.38 us
  blocking collectives: 38.7 us -> 0 us
  starting transfers between devices: 4.26 us -> 27.1 us
  local copies, waits for them, and re-layouts: 43.5 us -> 54.9 us
  waiting for transfers between devices: 24.9 us -> 20 us
    unnamed x6 -> x5, other arithmetic: 47.7 us -> 0.27 us
    dynamic_update_slice x0 -> x8, local copies, waits for them, and re-layouts: none -> 39.2 us  [tables_direct(): lax.dynamic_update_slice_in_dim(next_value, back, passed, axis=0)]
    all_to_all x1 -> x0, blocking collectives: 38.7 us -> none  [local(): lax.all_to_all(packed, 'row', split_axis=2, concat_axis=1, tiled=True)]
    unnamed x21 -> x20, local copies, waits for them, and re-layouts: 20 us -> 2.68 us
    ppermute x0 -> x7, starting transfers between devices: none -> 11.5 us  [tables_direct(): back = jax.lax.ppermute(met_up, axis_name=mesh_ax, perm=block_list)]
    all_to_all x1, starting transfers between devices: 4.26 us -> 15.6 us  [local(): lax.all_to_all(derivative_lines, 'row', split_axis=1, concat_axis=2, tile...]
    all_to_all x1 -> x0, local copies, waits for them, and re-layouts: 10.6 us -> none  [local(): lax.all_to_all(packed, 'row', split_axis=2, concat_axis=1, tiled=True)]
    all_to_all x1, waiting for transfers between devices: 24.9 us -> 14.6 us  [local(): lax.all_to_all(derivative_lines, 'row', split_axis=1, concat_axis=2, tile...]
  transfers between devices with their start and end apart: 1 -> 8, of which waited for: 1 -> 3; matrix products, arithmetic and copies ran while one was open for 3% -> 35% of each run, Pallas kernels for 0% -> 0%
where the time goes in v1:
time: 114 us; the launch traced here: 113 us
  local copies, waits for them, and re-layouts  54.9 us (48%)
  starting transfers between devices  27.1 us (24%)
  waiting for transfers between devices  20 us (18%)
  other arithmetic  5.38 us (5%)
  matrix products  4.76 us (4%)
    dynamic_update_slice x8, local copies, waits for them, and re-layouts, tables_direct(): lax.dynamic_update_slice_in_dim(next_value, back, passed, axis=0)  39.2 us
    all_to_all x1, starting transfers between devices, local(): lax.all_to_all(derivative_lines, 'row', split_axis=1, concat_axis=2, tile...  15.6 us
    all_to_all x1, waiting for transfers between devices, local(): lax.all_to_all(derivative_lines, 'row', split_axis=1, concat_axis=2, tile...  14.6 us
    ppermute x7, starting transfers between devices, tables_direct(): back = jax.lax.ppermute(met_up, axis_name=mesh_ax, perm=block_list)  11.5 us
    ppermute x7, waiting for transfers between devices, tables_direct(): back = jax.lax.ppermute(met_up, axis_name=mesh_ax, perm=block_list)  5.4 us
    dot_general x1, matrix products, compact_last(): jnp.einsum('...bj,jk->...bk', blocks, block_weights(count), precision=lax...  3.51 us
    neg x1, other arithmetic, local(): return -(derivative_x + derivative_y)  3.28 us
    unnamed x20, local copies, waits for them, and re-layouts  2.68 us
  transfers between devices with their start and end apart: 8, of which 3 were waited for; matrix products, arithmetic and copies ran while one was open for 35% of the time, Pallas kernels for 0%

profile of v1, /device:TPU:0, one launch (start us, length us, event | category | flops | bytes accessed | tf_op | source)
XLA Modules:
  0.0 112.6 jit_solution(368019086716041924)
XLA Ops:
  2.7 2.1 %copy.18 = f32[1,32,5,2048]{3,2,1,0:T(8,128)} copy(f32[1,32,5,2048]{3,1,2,0:T(8,128)S(1)} %bitcast_dynamic-update-slice_fusion.5) | data formatting | bytes 2621440 | tf_op jit(solution)/shard_map/stack | solution.py:113
  4.8 1.8 %reshape_reshape.3 = f32[1,32,8,1280]{3,2,1,0:T(8,128)S(1)} reshape(f32[1,32,5,2048]{3,2,1,0:T(8,128)} %copy.18) | data formatting | bytes 2621440 | tf_op jit(solution)/shard_map/reshape;reshape | solution.py:10
  6.7 1.6 %dynamic-slice_bitcast_fusion = (f32[1,1,32,1280]{3,0,2,1:T(1,128)}, f32[1,1,32,1280]{3,0,2,1:T(1,128)}, f32[1,1,32,1280]{3,0,2,1:T(1,128)}, f32[1,1,32,1280]{3,...) fusion(f32[1,32,8,1280]{3,2,1,0:T(8,128)S(1)} %reshape_reshape.3, ...), kind=kLoop, calls=%fused_computation.33 | loop fusion | bytes 2293788 | tf_op jit(solution)/shard_map/jit(dynamic_index_in_dim)/dynamic_slice | solution.py:27
  8.3 3.0 %collective-permute-start.1 = (f32[1,1,32,1280]{3,0,2,1:T(1,128)S(1)}, f32[1,1,32,1280]{3,0,2,1:T(1,128)}, u32[]{:S(2)}, u32[]{:S(2)}) collective-permute-start(f32[1,1,32,1280]{3,0,2,1:T(1,128)S(1)} %get-tuple-element.18), channel_id=1, source_target_pairs={{0,8},{4,12},{8,16},{12,20},{16,24},{20,28},{24,0},{28,4},{1,9},{5... | collective-permute-start | bytes 491528 | tf_op jit(solution)/shard_map/ppermute | solution.py:31
  11.3 1.5 %collective-permute-start = (f32[1,1,32,1280]{3,0,2,1:T(1,128)S(1)}, f32[1,1,32,1280]{3,0,2,1:T(1,128)}, u32[]{:S(2)}, u32[]{:S(2)}) collective-permute-start(f32[1,1,32,1280]{3,0,2,1:T(1,128)S(1)} %get-tuple-element.19), channel_id=1, source_target_pairs={{0,4},{4,8},{8,12},{12,16},{16,20},{20,24},{24,28},{28,0},{1,5},{5... | collective-permute-start | bytes 491528 | tf_op jit(solution)/shard_map/ppermute | solution.py:31
  12.8 2.0 %collective-permute-start.4 = (f32[1,1,32,1280]{3,0,2,1:T(1,128)}, f32[1,1,32,1280]{3,0,2,1:T(1,128)}, u32[]{:S(2)}, u32[]{:S(2)}) collective-permute-start(f32[1,1,32,1280]{3,0,2,1:T(1,128)} %get-tuple-element.15), channel_id=1, source_target_pairs={{0,20},{4,24},{8,28},{12,0},{16,4},{20,8},{24,12},{28,16},{1,21},{... | collective-permute-start | bytes 491528 | tf_op jit(solution)/shard_map/ppermute | solution.py:31
  15.8 2.6 %collective-permute-start.3 = (f32[1,1,32,1280]{3,0,2,1:T(1,128)}, f32[1,1,32,1280]{3,0,2,1:T(1,128)}, u32[]{:S(2)}, u32[]{:S(2)}) collective-permute-start(f32[1,1,32,1280]{3,0,2,1:T(1,128)} %get-tuple-element.16), channel_id=1, source_target_pairs={{0,16},{4,20},{8,24},{12,28},{16,0},{20,4},{24,8},{28,12},{1,17},{... | collective-permute-start | bytes 491528 | tf_op jit(solution)/shard_map/ppermute | solution.py:31
  18.4 1.5 %collective-permute-start.5 = (f32[1,1,32,1280]{3,0,2,1:T(1,128)}, f32[1,1,32,1280]{3,0,2,1:T(1,128)}, u32[]{:S(2)}, u32[]{:S(2)}) collective-permute-start(f32[1,1,32,1280]{3,0,2,1:T(1,128)} %get-tuple-element.14), channel_id=1, source_target_pairs={{0,24},{4,28},{8,0},{12,4},{16,8},{20,12},{24,16},{28,20},{1,25},{... | collective-permute-start | bytes 491528 | tf_op jit(solution)/shard_map/ppermute | solution.py:31
  19.8 3.4 %collective-permute-done = f32[1,1,32,1280]{3,0,2,1:T(1,128)} collective-permute-done((f32[1,1,32,1280]{3,0,2,1:T(1,128)S(1)}, f32[1,1,32,1280]{3,0,2,1:T(1,128)}, u32[]{:S(2)}, u32[]{:S(2)}) %collective-permute-start) | collective-permute-done | bytes 163872 | tf_op jit(solution)/shard_map/ppermute | solution.py:31
  23.2 5.5 %dynamic_update_slice.21 = f32[8,1,32,1280]{3,0,2,1:T(8,128)S(1)} dynamic-update-slice(f32[8,1,32,1280]{3,0,2,1:T(8,128)S(1)} %bitcast.119, f32[1,1,32,1280]{3,0,2,1:T(1,128)} %collective-permute-done, s32[]{:T(128)S(6)} %select_n.105, s32[]{:T(128)} %constant.107.clone.1, s32[]{:T(128)} %constant.107.clone.1, s32[]{:T(128)} %constant.107.clone.1) | dynamic-update-slice | bytes 327684 | tf_op jit(solution)/shard_map/dynamic_update_slice | solution.py:32
  28.7 5.6 %dynamic_update_slice.22 = f32[8,1,32,1280]{3,0,2,1:T(8,128)S(1)} dynamic-update-slice(f32[8,1,32,1280]{3,0,2,1:T(8,128)S(1)} %dynamic_update_slice.21, f32[1,1,32,1280]{3,0,2,1:T(1,128)} %collective-permute-done.1, s32[]{:T(128)S(6)} %select_n.109, s32[]{:T(128)} %constant.107.clone.1, s32[]{:T(128)} %constant.107.clone.1, s32[]{:T(128)} %constant.107.clone.1) | dynamic-update-slice | bytes 327684 | tf_op jit(solution)/shard_map/dynamic_update_slice | solution.py:32
  34.3 2.0 %collective-permute-done.2 = f32[1,1,32,1280]{3,0,2,1:T(1,128)} collective-permute-done((f32[1,1,32,1280]{3,0,2,1:T(1,128)}, f32[1,1,32,1280]{3,0,2,1:T(1,128)}, u32[]{:S(2)}, u32[]{:S(2)}) %collective-permute-start.2) | collective-permute-done | bytes 163872 | tf_op jit(solution)/shard_map/ppermute | solution.py:31
  36.3 5.5 %dynamic_update_slice.23 = f32[8,1,32,1280]{3,0,2,1:T(8,128)S(1)} dynamic-update-slice(f32[8,1,32,1280]{3,0,2,1:T(8,128)S(1)} %dynamic_update_slice.22, f32[1,1,32,1280]{3,0,2,1:T(1,128)} %collective-permute-done.2, s32[]{:T(128)S(6)} %select_n.113, s32[]{:T(128)} %constant.107.clone.1, s32[]{:T(128)} %constant.107.clone.1, s32[]{:T(128)} %constant.107.clone.1) | dynamic-update-slice | bytes 327684 | tf_op jit(solution)/shard_map/dynamic_update_slice | solution.py:32
  41.8 5.6 %dynamic_update_slice.24 = f32[8,1,32,1280]{3,0,2,1:T(8,128)S(1)} dynamic-update-slice(f32[8,1,32,1280]{3,0,2,1:T(8,128)S(1)} %dynamic_update_slice.23, f32[1,1,32,1280]{3,0,2,1:T(1,128)} %collective-permute-done.3, s32[]{:T(128)S(6)} %select_n.117, s32[]{:T(128)} %constant.107.clone.1, s32[]{:T(128)} %constant.107.clone.1, s32[]{:T(128)} %constant.107.clone.1) | dynamic-update-slice | bytes 327684 | tf_op jit(solution)/shard_map/dynamic_update_slice | solution.py:32
  47.4 5.6 %dynamic_update_slice.25 = f32[8,1,32,1280]{3,0,2,1:T(8,128)S(1)} dynamic-update-slice(f32[8,1,32,1280]{3,0,2,1:T(8,128)S(1)} %dynamic_update_slice.24, f32[1,1,32,1280]{3,0,2,1:T(1,128)} %collective-permute-done.4, s32[]{:T(128)S(6)} %select_n.121, s32[]{:T(128)} %constant.107.clone.1, s32[]{:T(128)} %constant.107.clone.1, s32[]{:T(128)} %constant.107.clone.1) | dynamic-update-slice | bytes 327684 | tf_op jit(solution)/shard_map/dynamic_update_slice | solution.py:32
  53.0 5.6 %dynamic_update_slice.26 = f32[8,1,32,1280]{3,0,2,1:T(8,128)S(1)} dynamic-update-slice(f32[8,1,32,1280]{3,0,2,1:T(8,128)S(1)} %dynamic_update_slice.25, f32[1,1,32,1280]{3,0,2,1:T(1,128)} %collective-permute-done.5, s32[]{:T(128)S(6)} %select_n.125, s32[]{:T(128)} %constant.107.clone.1, s32[]{:T(128)} %constant.107.clone.1, s32[]{:T(128)} %constant.107.clone.1) | dynamic-update-slice | bytes 327684 | tf_op jit(solution)/shard_map/dynamic_update_slice | solution.py:32
  58.5 5.6 %dynamic_update_slice.27 = f32[8,1,32,1280]{3,0,2,1:T(8,128)S(1)} dynamic-update-slice(f32[8,1,32,1280]{3,0,2,1:T(8,128)S(1)} %dynamic_update_slice.26, f32[1,1,32,1280]{3,0,2,1:T(1,128)} %collective-permute-done.6, s32[]{:T(128)S(6)} %select_n.129, s32[]{:T(128)} %constant.107.clone.1, s32[]{:T(128)} %constant.107.clone.1, s32[]{:T(128)} %constant.107.clone.1) | dynamic-update-slice | bytes 327684 | tf_op jit(solution)/shard_map/dynamic_update_slice | solution.py:32
  66.3 2.4 %copy.20 = f32[1,256,1280]{2,0,1:T(1,128)} copy(f32[1,256,1280]{2,1,0:T(8,128)S(1)} %convolution_bitcast_fusion) | data formatting | bytes 2621440 | tf_op jit(solution)/shard_map/...jc,ji->...ic/transpose | solution.py:85
  68.8 15.6 %all-to-all-start = ((f32[1,256,1280]{2,0,1:T(1,128)}), f32[1,256,1280]{2,0,1:T(1,128)S(1)}, u32[]{:S(2)}, u32[]{:S(2)}) async-start(f32[1,256,1280]{2,0,1:T(1,128)} %copy.20), calls=%async_computation | async-start | bytes 2621440 | tf_op jit(solution)/shard_map/all_to_all | solution.py:133
  85.8 3.5 %convolution_bitcast_fusion.1 = f32[5,1,32,16,384]{4,3,2,0,1:T(8,128)S(1)} fusion(f32[5,32,16,128]{3,2,1,0:T(8,128)S(1)} %bitcast_dynamic-update-slice_fusion, f32[128,384,1,1]{1,0,3,2:T(8,128)S(1)} %copy-done.4), kind=kOutput, calls=%fused_computation.1 | convolution fusion | flops 1509949440 | bytes 5439488 | tf_op jit(solution)/shard_map/...bj,jk->...bk/dot_general | solution.py:70
  91.3 14.6 %all-to-all-done = f32[1,256,1280]{2,0,1:T(1,128)S(1)} async-done(((f32[1,256,1280]{2,0,1:T(1,128)}), f32[1,256,1280]{2,0,1:T(1,128)S(1)}, u32[]{:S(2)}, u32[]{:S(2)}) %all-to-all-start) | async-done | bytes 1310752 | tf_op jit(solution)/shard_map/all_to_all | solution.py:133
  105.9 1.9 %copy.31 = f32[1,8,32,1280]{3,1,2,0:T(8,128)} copy(f32[1,8,32,1280]{3,0,2,1:T(1,128)S(1)} %bitcast.120) | data formatting | bytes 2621440 | tf_op jit(solution)/shard_map/all_to_all | solution.py:133
  107.8 1.5 %reshape.143 = f32[1,32,5,2048]{3,2,1,0:T(8,128)S(1)} reshape(f32[1,32,8,1280]{3,2,1,0:T(8,128)} %bitcast.122) | data formatting | bytes 2621440 | tf_op jit(solution)/shard_map/reshape | solution.py:134
  109.3 3.3 %fusion.1 = f32[5,1,32,2048]{3,2,1,0:T(8,128)} fusion(f32[5,1,32,2048]{3,2,1,0:T(8,128)} %reshape.141, f32[1,32,5,2048]{3,2,1,0:T(8,128)S(1)} %reshape.143), kind=kLoop, calls=%fused_computation.5 | loop fusion | flops 655360 | bytes 3932160 | tf_op jit(solution)/shard_map/neg | solution.py:135
  (41 shorter events, 9.0 us)
Async XLA Ops:
  0.0 2.5 %copy-start = (f32[3,1,32,2048]{3,2,1,0:T(8,128)S(1)}, f32[3,1,32,2048]{3,2,1,0:T(8,128)}, u32[]{:S(2)}) copy-start(f32[3,1,32,2048]{3,2,1,0:T(8,128)} %param.6) | copy-start | bytes 2359300
  1.0 1.5 %copy-start.1 = (f32[1,32,2048]{2,1,0:T(8,128)S(1)}, f32[1,32,2048]{2,1,0:T(8,128)}, u32[]{:S(2)}) copy-start(f32[1,32,2048]{2,1,0:T(8,128)} %param.7) | copy-start | bytes 786436
  1.1 1.5 %copy-start.2 = (f32[1,32,2048]{2,1,0:T(8,128)S(1)}, f32[1,32,2048]{2,1,0:T(8,128)}, u32[]{:S(2)}) copy-start(f32[1,32,2048]{2,1,0:T(8,128)} %param.5) | copy-start | bytes 786436
  8.3 10.1 %collective-permute-start.1 = (f32[1,1,32,1280]{3,0,2,1:T(1,128)S(1)}, f32[1,1,32,1280]{3,0,2,1:T(1,128)}, u32[]{:S(2)}, u32[]{:S(2)}) collective-permute-start(f32[1,1,32,1280]{3,0,2,1:T(1,128)S(1)} %get-tuple-element.18), channel_id=1, source_target_pairs={{0,8},{4,12},{8,16},{12,20},{16,24},{20,28},{24,0},{28,4},{1,9},{5... | collective-permute-start | bytes 491528 | tf_op jit(solution)/shard_map/ppermute | solution.py:31
  11.3 11.9 %collective-permute-start = (f32[1,1,32,1280]{3,0,2,1:T(1,128)S(1)}, f32[1,1,32,1280]{3,0,2,1:T(1,128)}, u32[]{:S(2)}, u32[]{:S(2)}) collective-permute-start(f32[1,1,32,1280]{3,0,2,1:T(1,128)S(1)} %get-tuple-element.19), channel_id=1, source_target_pairs={{0,4},{4,8},{8,12},{12,16},{16,20},{20,24},{24,28},{28,0},{1,5},{5... | collective-permute-start | bytes 491528 | tf_op jit(solution)/shard_map/ppermute | solution.py:31
  12.8 34.5 %collective-permute-start.4 = (f32[1,1,32,1280]{3,0,2,1:T(1,128)}, f32[1,1,32,1280]{3,0,2,1:T(1,128)}, u32[]{:S(2)}, u32[]{:S(2)}) collective-permute-start(f32[1,1,32,1280]{3,0,2,1:T(1,128)} %get-tuple-element.15), channel_id=1, source_target_pairs={{0,20},{4,24},{8,28},{12,0},{16,4},{20,8},{24,12},{28,16},{1,21},{... | collective-permute-start | bytes 491528 | tf_op jit(solution)/shard_map/ppermute | solution.py:31
  14.9 21.4 %collective-permute-start.2 = (f32[1,1,32,1280]{3,0,2,1:T(1,128)}, f32[1,1,32,1280]{3,0,2,1:T(1,128)}, u32[]{:S(2)}, u32[]{:S(2)}) collective-permute-start(f32[1,1,32,1280]{3,0,2,1:T(1,128)} %get-tuple-element.17), channel_id=1, source_target_pairs={{0,12},{4,16},{8,20},{12,24},{16,28},{20,0},{24,4},{28,8},{1,13},{... | collective-permute-start | bytes 491528 | tf_op jit(solution)/shard_map/ppermute | solution.py:31
  15.8 26.0 %collective-permute-start.3 = (f32[1,1,32,1280]{3,0,2,1:T(1,128)}, f32[1,1,32,1280]{3,0,2,1:T(1,128)}, u32[]{:S(2)}, u32[]{:S(2)}) collective-permute-start(f32[1,1,32,1280]{3,0,2,1:T(1,128)} %get-tuple-element.16), channel_id=1, source_target_pairs={{0,16},{4,20},{8,24},{12,28},{16,0},{20,4},{24,8},{28,12},{1,17},{... | collective-permute-start | bytes 491528 | tf_op jit(solution)/shard_map/ppermute | solution.py:31
  18.4 34.6 %collective-permute-start.5 = (f32[1,1,32,1280]{3,0,2,1:T(1,128)}, f32[1,1,32,1280]{3,0,2,1:T(1,128)}, u32[]{:S(2)}, u32[]{:S(2)}) collective-permute-start(f32[1,1,32,1280]{3,0,2,1:T(1,128)} %get-tuple-element.14), channel_id=1, source_target_pairs={{0,24},{4,28},{8,0},{12,4},{16,8},{20,12},{24,16},{28,20},{1,25},{... | collective-permute-start | bytes 491528 | tf_op jit(solution)/shard_map/ppermute | solution.py:31
  23.2 35.3 %collective-permute-start.6 = (f32[1,1,32,1280]{3,0,2,1:T(1,128)}, f32[1,1,32,1280]{3,0,2,1:T(1,128)}, u32[]{:S(2)}, u32[]{:S(2)}) collective-permute-start(f32[1,1,32,1280]{3,0,2,1:T(1,128)} %get-tuple-element.13), channel_id=1, source_target_pairs={{0,28},{4,0},{8,4},{12,8},{16,12},{20,16},{24,20},{28,24},{1,29},{... | collective-permute-start | bytes 491528 | tf_op jit(solution)/shard_map/ppermute | solution.py:31
  64.1 1.0 copy-start.3
  68.8 37.1 %all-to-all-start = ((f32[1,256,1280]{2,0,1:T(1,128)}), f32[1,256,1280]{2,0,1:T(1,128)S(1)}, u32[]{:S(2)}, u32[]{:S(2)}) async-start(f32[1,256,1280]{2,0,1:T(1,128)} %copy.20), calls=%async_computation | async-start | bytes 2621440 | tf_op jit(solution)/shard_map/all_to_all | solution.py:133
  84.8 0.9 copy-start.4
